TPU v7x, 512 devices: a whole 4x4x16 slice. The times are simulated.
512 devices in a mesh: grp: 4 (over y), seq: 32 (over z, core), mp: 4 (over x).
Axes of the slice: x: 4, y: 4, z: 16, core: 2. Of those that a mesh axis runs over, the one named last changes fastest.
Arguments:
- queries: bfloat16 [4, 4096, 2048], P('grp', 'seq', 'mp'), may hold values from -16 to 16
- d_out: bfloat16 [4, 4096, 2048], P('grp', 'seq', 'mp'), may hold values from -6 to 6
- neighbour_kv: bfloat16 [4, 256, 128, 2, 2048], P('grp', 'seq', None, None, 'mp'), may hold values from -16 to 16
- target: int32 [4, 256], P('grp', 'seq'), may hold values from -1 to 127, as said below
- bias: float32 [16, 191], P('mp'), may hold values from -6 to 6
Outputs:
- attended: bfloat16 [4, 4096, 2048], P('grp', 'seq', 'mp')
- d_query: bfloat16 [4, 4096, 2048], P('grp', 'seq', 'mp')
- d_kv: bfloat16 [4, 256, 128, 2, 2048], P('grp', 'seq', None, None, 'mp')
- d_bias: float32 [16, 191], P('mp')
Inputs may be any that keep to these rules, and one draw needn't show every extreme that they name: `target`: in each group every entry 0..127 stands in exactly one slot and -1 marks an empty slot. The slots of one index of seq hold at most 1 entries e with the same e // 4, and some index reaches that; some index of seq holds 8 entries.
All inputs are finite; a program needn't handle non-finite values.
Results may differ from a plain program's by a relative error of at most 0.011.
Values may be sent and summed in bfloat16 or wider, within the bound.
No kernel may reach another device: no remote copies, remote signals or barrier semaphores. Data moves between devices by JAX's collectives and lax.ppermute only.
A program may use at most 128 MiB of HBM per device.

v0:
```python
import jax
import jax.numpy as jnp
from jax import lax
from jax.sharding import PartitionSpec as P

STRETCH = 64
NB_LEN = 128
SEQ_LEN = 2048


def passed_along(block, axis, distance):
    devices = range(lax.axis_size(axis))
    route = [(i - distance, i) for i in devices if i - distance in devices]
    return lax.ppermute(block, axis, route)


def bias_grid(lookup, row_count, col_count):
    head_num = lookup.shape[0]
    span = row_count + col_count
    padded = jnp.pad(lookup, ((0, 0), (0, 1)))
    flattened = jnp.tile(padded, (1, row_count))
    flattened = jnp.pad(flattened, ((0, 0), (0, row_count)))
    shaped = flattened.reshape(head_num, row_count, span + 1)[:, :, :col_count]
    return shaped[:, :, ::-1]


def bias_fold(grads):
    head_num, row_count, col_count = grads.shape
    turned = grads[:, :, ::-1]
    padded = jnp.pad(turned, ((0, 0), (0, 0), (0, row_count)))
    flattened = padded.reshape(head_num, row_count * (row_count + col_count))
    flattened = flattened[:, : row_count * (row_count + col_count - 1)]
    return jnp.sum(flattened.reshape(head_num, row_count, row_count + col_count - 1), axis=1)


def take_rows(table, index, valid):
    rows = jnp.take(table, index, axis=0)
    shape = (valid.shape[0],) + (1,) * (rows.ndim - 1)
    return jnp.where(valid.reshape(shape), rows, jnp.zeros((), rows.dtype))


def exchange(block):
    return lax.all_to_all(block, "seq", split_axis=0, concat_axis=0, tiled=True)


def local(queries, d_out, neighbour_kv, target, bias):
    tok_rows = queries.shape[1]
    width_dev = queries.shape[2]
    head_count = bias.shape[0]
    head_depth = width_dev // head_count
    stretch_count = tok_rows // STRETCH
    per_owner = 2 * stretch_count
    shard_count = lax.axis_size("seq")
    my_index = lax.axis_index("seq")
    group_rows = tok_rows * shard_count
    seq_stretches = min(SEQ_LEN, group_rows) // STRETCH
    scale_factor = head_depth ** (-0.5)
    bias_rows = bias_grid(bias, STRETCH, NB_LEN).transpose(1, 0, 2)
    row_ids = jnp.arange(STRETCH)
    q_all = lax.all_gather(queries[0], "seq", axis=0, tiled=True)
    g_all = lax.all_gather(d_out[0], "seq", axis=0, tiled=True)
    my_targets = target[0]
    slot_count = my_targets.shape[0]
    is_used = my_targets >= 0
    entry = jnp.where(is_used, my_targets, 0)
    stretch_of = entry // 2
    win_rows = stretch_of[:, None] * STRETCH + (STRETCH - 1) + row_ids[None, :]
    in_group = win_rows < group_rows
    win_rows = jnp.minimum(win_rows.reshape(-1), group_rows - 1)
    q_win = jnp.take(q_all, win_rows, axis=0).reshape(slot_count, STRETCH, width_dev)
    g_win = jnp.take(g_all, win_rows, axis=0).reshape(slot_count, STRETCH, width_dev)
    live_slot = (row_ids[None, :] == 0) | ((stretch_of[:, None] + 1) % seq_stretches != 0)
    q_keep = is_used[:, None] & in_group
    q_slots = jnp.where(q_keep[:, :, None], q_win, jnp.zeros((), q_win.dtype))
    g_slots = jnp.where((q_keep & live_slot)[:, :, None], g_win, jnp.zeros((), g_win.dtype))
    q_slots = q_slots.reshape(slot_count, STRETCH, head_count, head_depth)
    g_slots = g_slots.reshape(slot_count, STRETCH, head_count, head_depth)
    stored = neighbour_kv[0]
    key_rows = stored[:, :, 0].reshape(slot_count, NB_LEN, head_count, head_depth)
    value_rows = stored[:, :, 1].reshape(slot_count, NB_LEN, head_count, head_depth)
    scores = jnp.einsum("sihd,sjhd->sihj", q_slots, key_rows, preferred_element_type=jnp.float32)
    scores = scores * scale_factor + bias_rows[None]
    peak_val = jnp.max(scores, axis=-1)
    weights = jnp.exp(scores - peak_val[..., None])
    row_total = jnp.sum(weights, axis=-1)
    partial_value = jnp.einsum(
        "sihj,sjhd->sihd",
        weights.astype(jnp.bfloat16),
        value_rows,
        preferred_element_type=jnp.float32,
    )
    owner_of = jnp.where(is_used, my_targets // per_owner, -1)
    owner_match = owner_of[None, :] == jnp.arange(shard_count)[:, None]
    send_slot = jnp.argmax(owner_match, axis=1)
    send_has = jnp.any(owner_match, axis=1)
    part_send = take_rows(
        partial_value.astype(jnp.bfloat16).reshape(slot_count, STRETCH, width_dev),
        send_slot,
        send_has,
    )
    slot_stats = jnp.concatenate(
        [
            jnp.stack([peak_val, row_total], axis=1).reshape(slot_count, -1),
            (entry + 1).astype(jnp.float32)[:, None],
        ],
        axis=1,
    )
    stat_send = take_rows(slot_stats, send_slot, send_has)
    part_recv = exchange(part_send)
    stat_recv = exchange(stat_send)
    own_entries = my_index * per_owner + jnp.arange(per_owner)
    sent_ids = stat_recv[:, -1].astype(jnp.int32) - 1
    where_held = sent_ids[None, :] == own_entries[:, None]
    held_by = jnp.argmax(where_held, axis=1)
    parts_own = jnp.take(part_recv, held_by, axis=0).astype(jnp.float32)
    parts_own = parts_own.reshape(stretch_count, 2, STRETCH, head_count, head_depth)
    stats_own = jnp.take(stat_recv[:, :-1], held_by, axis=0)
    stats_own = stats_own.reshape(stretch_count, 2, 2, STRETCH, head_count)
    peaks_own = stats_own[:, :, 0]
    totals_own = stats_own[:, :, 1]
    stretch_ids = my_index * stretch_count + jnp.arange(stretch_count)
    is_live = (row_ids[None, :] == 0) | ((stretch_ids[:, None] + 1) % seq_stretches != 0)
    live_rows = is_live.astype(jnp.float32)
    top_peak = jnp.max(peaks_own, axis=1)
    factor = jnp.exp(peaks_own - top_peak[:, None])
    denominator = jnp.sum(factor * totals_own, axis=1)
    combined = jnp.sum(factor[..., None] * parts_own, axis=1) / denominator[..., None]
    combined = combined * live_rows[:, :, None, None]
    att_win = combined.astype(jnp.bfloat16).reshape(tok_rows, width_dev)
    att_before = passed_along(att_win[tok_rows - STRETCH :], "seq", 1)
    g_dot = jnp.einsum(
        "sihd,sihd->sih",
        g_slots.astype(jnp.float32),
        partial_value,
        precision=lax.Precision.HIGHEST,
    )
    mine = jnp.stack([peak_val, row_total, g_dot], axis=1)
    shared = jnp.concatenate(
        [
            mine.reshape(slot_count, -1),
            jnp.where(is_used, entry + 1, 0).astype(jnp.float32)[:, None],
        ],
        axis=1,
    )
    shared_all = lax.all_gather(shared, "seq", tiled=True)
    partner = entry + 1 - 2 * (entry % 2)
    partner_at = jnp.argmax(
        shared_all[None, :, -1] == (partner + 1).astype(jnp.float32)[:, None], axis=1
    )
    theirs = jnp.take(shared_all[:, :-1], partner_at, axis=0).reshape(mine.shape)
    both_peak = jnp.maximum(mine[:, 0], theirs[:, 0])
    mine_f = jnp.exp(mine[:, 0] - both_peak)
    theirs_f = jnp.exp(theirs[:, 0] - both_peak)
    both_total = mine_f * mine[:, 1] + theirs_f * theirs[:, 1]
    lse_slots = both_peak + jnp.log(both_total)
    dd_slots = (mine_f * mine[:, 2] + theirs_f * theirs[:, 2]) / both_total
    dd_slots = jnp.where(is_used[:, None, None], dd_slots, 0.0)
    prob_full = jnp.exp(scores - lse_slots[..., None])
    prob_low = prob_full.astype(jnp.bfloat16)
    grad_prob = jnp.einsum(
        "sihd,sjhd->sihj", g_slots, value_rows, preferred_element_type=jnp.float32
    )
    grad_scores = prob_full * (grad_prob - dd_slots[..., None])
    scores_low = grad_scores.astype(jnp.bfloat16)
    grad_rows = (
        jnp.einsum("sihj,sjhd->sihd", scores_low, key_rows, preferred_element_type=jnp.float32)
        * scale_factor
    )
    mix_probs = jnp.stack([scores_low, prob_low], axis=1)
    mix_rows = jnp.stack([q_slots, g_slots], axis=1)
    grad_kv = jnp.einsum(
        "sxihj,sxihd->sjxhd", mix_probs, mix_rows, preferred_element_type=jnp.float32
    )
    kv_scale = jnp.array([scale_factor, 1.0], jnp.float32)[None, None, :, None, None]
    d_kv = (grad_kv * kv_scale).astype(jnp.bfloat16).reshape(slot_count, NB_LEN, 2, width_dev)
    bias_part = bias_fold(jnp.sum(grad_scores, axis=0).transpose(1, 0, 2))
    dq_rows = jnp.zeros((shard_count, stretch_count, STRETCH, width_dev), jnp.bfloat16)
    dq_owner = jnp.where(is_used, owner_of, shard_count)
    dq_rows = dq_rows.at[dq_owner, stretch_of % stretch_count].set(
        grad_rows.astype(jnp.bfloat16).reshape(slot_count, STRETCH, width_dev), mode="drop"
    )
    grad_win = lax.psum_scatter(dq_rows, "seq", scatter_dimension=0, tiled=True)
    grad_win = grad_win.reshape(tok_rows, width_dev)
    grad_before = passed_along(grad_win[tok_rows - STRETCH :], "seq", 1)
    attended = jnp.concatenate([att_before[1:], att_win[: tok_rows - STRETCH + 1]])
    d_query = jnp.concatenate([grad_before[1:], grad_win[: tok_rows - STRETCH + 1]])
    raw_sum = lax.psum(lax.psum(bias_part, "seq"), "grp")
    squares = lax.psum(jnp.sum(raw_sum * raw_sum), "mp")
    d_bias = raw_sum * jnp.minimum(1.0, 1.0 / jnp.sqrt(squares + 1e-12))
    return (attended[None], d_query[None], d_kv[None], d_bias)


def solution(mesh):
    in_specs = (
        P("grp", "seq", "mp"),
        P("grp", "seq", "mp"),
        P("grp", "seq", None, None, "mp"),
        P("grp", "seq"),
        P("mp", None),
    )
    out_specs = (
        P("grp", "seq", "mp"),
        P("grp", "seq", "mp"),
        P("grp", "seq", None, None, "mp"),
        P("mp", None),
    )
    return jax.shard_map(local, mesh=mesh, in_specs=in_specs, out_specs=out_specs, check_vma=False)
```

profile of v0, /device:TPU:97, one launch (start us, length us, event | category | flops | bytes accessed | tf_op | source)
XLA Modules:
  0.0 430.7 jit_solution(3914705341878619618)
XLA Ops:
  7.2 0.7 all-gather.7.cloned.1.call-update
  8.0 0.7 all-gather.5.cloned.1.call-update
  8.7 0.7 fusion.50
  9.5 0.7 copy.86
  10.2 0.7 pad.12
  11.6 3.8 copy.83
  16.4 2.8 fusion.60
  19.2 67.8 %all-gather.7.cloned.1.call-done = bf16[1,4096,512]{2,1,0:T(8,128)(2,1)} async-done(((bf16[1,128,512]{2,1,0:T(8,128)(2,1)}), bf16[1,4096,512]{2,1,0:T(8,128)(2,1)}) %all-gather.7.cloned.1.call-update) | async-done | bytes 4194320 | tf_op jit(solution)/shard_map/all_gather | solution.py:61
  86.9 4.7 %gather_fusion.6 = bf16[512,512]{1,0:T(8,128)(2,1)S(1)} fusion(bf16[4096,512]{1,0:T(8,128)(2,1)} %bitcast.151, s32[1024]{0:T(1024)S(1)} %pad_clamp_fusion.3), kind=kCustom, calls=%fused_computation.1.clone | custom fusion | bytes 1050624 | tf_op jit(solution)/shard_map/jit(_take)/gather | solution.py:71
  91.7 68.3 %all-gather.5.cloned.1.call-done = bf16[1,4096,512]{2,1,0:T(8,128)(2,1)} async-done(((bf16[1,128,512]{2,1,0:T(8,128)(2,1)}), bf16[1,4096,512]{2,1,0:T(8,128)(2,1)}) %all-gather.5.cloned.1.call-update) | async-done | bytes 4194320 | tf_op jit(solution)/shard_map/all_gather | solution.py:60
  160.0 4.7 %gather_fusion.5 = bf16[512,512]{1,0:T(8,128)(2,1)S(1)} fusion(bf16[4096,512]{1,0:T(8,128)(2,1)} %bitcast.152, s32[1024]{0:T(1024)S(1)} %pad_clamp_fusion.3), kind=kCustom, calls=%fused_computation.clone | custom fusion | bytes 1050624 | tf_op jit(solution)/shard_map/jit(_take)/gather | solution.py:70
  164.9 1.0 reshape.666
  165.8 0.9 reshape.662
  166.8 1.7 fusion.62
  168.5 3.2 fusion.9
  172.1 29.3 %all_gather.11 = f32[256,769]{1,0:T(8,128)S(1)} all-gather(f32[8,769]{1,0:T(8,128)S(1)} %pad_maximum_fusion.3), channel_id=1, replica_groups=mesh['grp'=4,'seq'=32,'mp'=4] {'seq'}, dimensions={0}, use_global_device_ids=true | all-gather | bytes 812064 | tf_op jit(solution)/shard_map/all_gather | solution.py:145
  201.5 0.7 iota_reduce_fusion
  202.3 1.1 copy.142
  203.7 0.6 gather_fusion
  204.4 0.7 copy.89
  205.2 10.6 %all-to-all-start = ((f32[32,1,513]{2,1,0:T(1,128)}), f32[32,1,513]{2,1,0:T(1,128)S(1)}, u32[]{:S(2)}, u32[]{:S(2)}) async-start(f32[32,1,513]{2,1,0:T(1,128)} %copy.89), calls=%async_computation | async-start | bytes 163840 | tf_op jit(solution)/shard_map/all_to_all | solution.py:43
  215.7 2.0 gather_fusion.2
  217.7 3.3 select_select_fusion
  221.1 0.9 slice.114
  222.0 1.7 gather_fusion.4
  224.2 3.4 all-to-all-done
  227.6 8.9 %all-to-all-start.1 = ((bf16[32,64,512]{2,1,0:T(8,128)(2,1)}), bf16[32,64,512]{2,1,0:T(8,128)(2,1)}, u32[]{:S(2)}, u32[]{:S(2)}) async-start(bf16[32,64,512]{2,1,0:T(8,128)(2,1)} %select_select_fusion), calls=%async_computation.1 | async-start | bytes 4194304 | tf_op jit(solution)/shard_map/all_to_all | solution.py:43
  236.7 1.9 fusion.3
  238.6 0.8 fusion.5
  239.7 2.4 broadcast_in_dim.191
  242.1 2.5 scatter_fusion
  245.0 0.8 copy-done.1
  245.8 0.9 fusion.61
  247.4 127.2 %psum.21 = f32[4,191]{1,0:T(4,128)S(1)} all-reduce(f32[4,191]{1,0:T(4,128)S(1)} %reduce_sum.58), channel_id=1, replica_groups=mesh['grp'=4,'seq'=32,'mp'=4] {'seq'}, use_global_device_ids=true, to_apply=%region_13.15 | all-reduce | flops 764 | bytes 6112 | tf_op jit(solution)/shard_map/psum | solution.py:187
  374.6 8.4 %psum.22 = f32[4,191]{1,0:T(4,128)S(1)} all-reduce(f32[4,191]{1,0:T(4,128)S(1)} %psum.21), channel_id=1, replica_groups=mesh['grp'=4,'seq'=32,'mp'=4] {'grp'}, use_global_device_ids=true, to_apply=%region_14.16 | all-reduce | flops 764 | bytes 6112 | tf_op jit(solution)/shard_map/psum | solution.py:187
  383.0 0.6 multiply_reduce_fusion.1
  383.6 9.3 %psum.23 = f32[]{:T(128)} all-reduce(f32[]{:T(128)} %multiply_reduce_fusion.1), channel_id=1, replica_groups=mesh['grp'=4,'seq'=32,'mp'=4] {'mp'}, use_global_device_ids=true, to_apply=%region_16.18 | all-reduce | flops 1 | bytes 8 | tf_op jit(solution)/shard_map/psum | solution.py:188
  394.6 0.9 multiply_convert_fusion
  395.4 3.8 copy.108
  399.9 0.7 iota_reduce_fusion.2
  401.7 2.2 gather_fusion.3
  404.8 9.4 %collective-permute-start = (bf16[64,512]{1,0:T(8,128)(2,1)S(1)}, bf16[64,512]{1,0:T(8,128)(2,1)S(1)}, u32[]{:S(2)}, u32[]{:S(2)}) collective-permute-start(bf16[64,512]{1,0:T(8,128)(2,1)S(1)} %bitcast.173), channel_id=1, source_target_pairs={{0,4},{4,8},{8,12},{12,16},{16,20},{20,24},{24,28},{28,32},{32,36}... | collective-permute-start | bytes 196616 | tf_op jit(solution)/shard_map/ppermute | solution.py:14
  414.3 1.2 collective-permute-done
  415.6 0.8 slice_bitcast_fusion.1
  416.4 5.5 %collective-permute-start.1 = (bf16[64,512]{1,0:T(8,128)(2,1)S(1)}, bf16[64,512]{1,0:T(8,128)(2,1)S(1)}, u32[]{:S(2)}, u32[]{:S(2)}) collective-permute-start(bf16[64,512]{1,0:T(8,128)(2,1)S(1)} %slice_bitcast_fusion.1), channel_id=1, source_target_pairs={{0,4},{4,8},{8,12},{12,16},{16,20},{20,24},{24,28},{28,32},{32,36}... | collective-permute-start | bytes 196616 | tf_op jit(solution)/shard_map/ppermute | solution.py:14
  421.9 0.7 maximum_bitcast_fusion
  422.6 0.9 slice.120
  423.5 0.7 maximum_bitcast_fusion.1
  (111 shorter events, 8.3 us)
Async XLA Ops:
  7.2 4.4 %copy-start.6 = (bf16[1,8,128,2,512]{4,3,2,1,0:T(2,128)(2,1)S(1)}, bf16[1,8,128,2,512]{4,3,2,1,0:T(2,128)(2,1)}, u32[]{:S(2)}) copy-start(bf16[1,8,128,2,512]{4,3,2,1,0:T(2,128)(2,1)} %param.10) | copy-start | bytes 6291460
  7.2 79.8 %all-gather.7.cloned.1.call-start = ((), (), s32[]{:S(2)}) async-start(), calls=%async_computation.5 | async-start | bytes 4325376 | tf_op jit(solution)/shard_map/all_gather | solution.py:61
  7.9 152.1 %all-gather.5.cloned.1.call-start = ((), (), s32[]{:S(2)}) async-start(), calls=%async_computation.4 | async-start | bytes 4325376 | tf_op jit(solution)/shard_map/all_gather | solution.py:60
  11.6 3.8 copy-start.10
  164.9 3.6 copy-start.2
  166.8 1.7 copy-start.7
  201.4 0.9 copy-start.4
  205.2 22.5 %all-to-all-start = ((f32[32,1,513]{2,1,0:T(1,128)}), f32[32,1,513]{2,1,0:T(1,128)S(1)}, u32[]{:S(2)}, u32[]{:S(2)}) async-start(f32[32,1,513]{2,1,0:T(1,128)} %copy.89), calls=%async_computation | async-start | bytes 163840 | tf_op jit(solution)/shard_map/all_to_all | solution.py:43
  217.7 3.4 copy-start.5
  224.2 12.5 %copy-start.8 = (bf16[8,64,4,128]{3,2,1,0:T(4,128)(2,1)S(1)}, bf16[8,64,4,128]{3,2,1,0:T(4,128)(2,1)}, u32[]{:S(2)}) copy-start(bf16[8,64,4,128]{3,2,1,0:T(4,128)(2,1)} %reshape.666) | copy-start | bytes 1572868
  227.6 174.1 %all-to-all-start.1 = ((bf16[32,64,512]{2,1,0:T(8,128)(2,1)}), bf16[32,64,512]{2,1,0:T(8,128)(2,1)}, u32[]{:S(2)}, u32[]{:S(2)}) async-start(bf16[32,64,512]{2,1,0:T(8,128)(2,1)} %select_select_fusion), calls=%async_computation.1 | async-start | bytes 4194304 | tf_op jit(solution)/shard_map/all_to_all | solution.py:43
  236.6 179.0 %reduce-scatter.2.cloned.1.call-start = ((), (), s32[]{:S(2)}) async-start(), calls=%async_computation.3 | async-start | bytes 4325376 | tf_op jit(solution)/shard_map/reduce_scatter | solution.py:182
  238.6 1.0 copy-start
  244.6 1.2 copy-start.1
  244.6 148.3 %copy-start.3 = (bf16[512,512]{1,0:T(8,128)(2,1)S(1)}, bf16[512,512]{1,0:T(8,128)(2,1)}, u32[]{:S(2)}) copy-start(bf16[512,512]{1,0:T(8,128)(2,1)} %copy-done.2) | copy-start | bytes 1572868
  393.2 1.3 copy-start.9
  393.2 1.3 copy-start.11
  404.8 10.7 %collective-permute-start = (bf16[64,512]{1,0:T(8,128)(2,1)S(1)}, bf16[64,512]{1,0:T(8,128)(2,1)S(1)}, u32[]{:S(2)}, u32[]{:S(2)}) collective-permute-start(bf16[64,512]{1,0:T(8,128)(2,1)S(1)} %bitcast.173), channel_id=1, source_target_pairs={{0,4},{4,8},{8,12},{12,16},{16,20},{20,24},{24,28},{28,32},{32,36}... | collective-permute-start | bytes 196616 | tf_op jit(solution)/shard_map/ppermute | solution.py:14
  416.4 7.0 %collective-permute-start.1 = (bf16[64,512]{1,0:T(8,128)(2,1)S(1)}, bf16[64,512]{1,0:T(8,128)(2,1)S(1)}, u32[]{:S(2)}, u32[]{:S(2)}) collective-permute-start(bf16[64,512]{1,0:T(8,128)(2,1)S(1)} %slice_bitcast_fusion.1), channel_id=1, source_target_pairs={{0,4},{4,8},{8,12},{12,16},{16,20},{20,24},{24,28},{28,32},{32,36}... | collective-permute-start | bytes 196616 | tf_op jit(solution)/shard_map/ppermute | solution.py:14
Sparse Core Ops, SparseCore 0:
  10.1 76.7 all-gather.6
  89.1 70.8 all-gather.4
  244.8 153.5 reduce-scatter.1
where the time goes:
time: 432 us; the launch traced here: 431 us
  blocking collectives  174 us (40%)
  waiting for transfers between devices  142 us (33%)
  local copies, waits for them, and re-layouts  44 us (10%)
  starting transfers between devices  34.5 us (8%)
  between operations  15 us (3%)
  other arithmetic  12.3 us (3%)
  matrix products  8.49 us (2%)
    psum x2, blocking collectives, local(): raw_sum = lax.psum(lax.psum(bias_part, 'seq'), 'grp')  136 us
    all_gather x1, waiting for transfers between devices, local(): q_all = lax.all_gather(queries[0], 'seq', axis=0, tiled=True)  68.3 us
    all_gather x1, waiting for transfers between devices, local(): g_all = lax.all_gather(d_out[0], 'seq', axis=0, tiled=True)  67.8 us
    all_gather x1, blocking collectives, local(): shared_all = lax.all_gather(shared, 'seq', tiled=True)  29.3 us
    all_to_all x2, starting transfers between devices, exchange(): return lax.all_to_all(block, 'seq', split_axis=0, concat_axis=0, tiled=True)  19.5 us
    ppermute x2, starting transfers between devices, passed_along(): return lax.ppermute(block, axis, route)  14.9 us
    psum x1, blocking collectives, local(): squares = lax.psum(jnp.sum(raw_sum * raw_sum), 'mp')  9.29 us
    unnamed x29, local copies, waits for them, and re-layouts  8.74 us
  transfers between devices with their start and end apart: 7, of which 4 were waited for; matrix products, arithmetic and copies ran while one was open for 11% of the time, Pallas kernels for 0%

commit v1 on v0

--- a/solution.py
+++ b/solution.py
@@ -57,7 +57,9 @@
     scale_factor = head_depth ** (-0.5)
     bias_rows = bias_grid(bias, STRETCH, NB_LEN).transpose(1, 0, 2)
     row_ids = jnp.arange(STRETCH)
-    q_all = lax.all_gather(queries[0], "seq", axis=0, tiled=True)
+    q_all = jnp.concatenate(
+        lax.all_to_all(jnp.stack([queries[0]] * lax.axis_size("seq")), "seq", 0, 0), axis=0
+    )
     g_all = lax.all_gather(d_out[0], "seq", axis=0, tiled=True)
     my_targets = target[0]
     slot_count = my_targets.shape[0]

time: 432 us -> 505 us (1.17)
  waiting for transfers between devices: 142 us -> 197 us
  starting transfers between devices: 34.5 us -> 47.9 us
    all_gather x1, waiting for transfers between devices: 67.8 us -> 146 us  [local(): g_all = lax.all_gather(d_out[0], 'seq', axis=0, tiled=True)]
    all_gather x1 -> x0, waiting for transfers between devices: 68.3 us -> none  [local(): q_all = lax.all_gather(queries[0], 'seq', axis=0, tiled=True)]
    all_to_all x0 -> x1, waiting for transfers between devices: none -> 45.4 us  [local(): lax.all_to_all(jnp.stack([queries[0]] * lax.axis_size('seq')), 'seq', 0, 0)]
    all_to_all x0 -> x1, starting transfers between devices: none -> 14.9 us  [local(): lax.all_to_all(jnp.stack([queries[0]] * lax.axis_size('seq')), 'seq', 0, 0)]
  transfers between devices with their start and end apart: 7 -> 7, of which waited for: 4 -> 4; matrix products, arithmetic and copies ran while one was open for 11% -> 9% of each run, Pallas kernels for 0% -> 0%
where the time goes in v1:
time: 505 us; the launch traced here: 504 us
  waiting for transfers between devices  197 us (39%)
  blocking collectives  177 us (35%)
  starting transfers between devices  47.9 us (9%)
  local copies, waits for them, and re-layouts  46.1 us (9%)
  between operations  15.3 us (3%)
  other arithmetic  11.6 us (2%)
  matrix products  8.49 us (2%)
    all_gather x1, waiting for transfers between devices, local(): g_all = lax.all_gather(d_out[0], 'seq', axis=0, tiled=True)  146 us
    psum x2, blocking collectives, local(): raw_sum = lax.psum(lax.psum(bias_part, 'seq'), 'grp')  136 us
    all_to_all x1, waiting for transfers between devices, local(): lax.all_to_all(jnp.stack([queries[0]] * lax.axis_size('seq')), 'seq', 0, 0)  45.4 us
    all_gather x1, blocking collectives, local(): shared_all = lax.all_gather(shared, 'seq', tiled=True)  32.3 us
    all_to_all x2, starting transfers between devices, exchange(): return lax.all_to_all(block, 'seq', split_axis=0, concat_axis=0, tiled=True)  17.8 us
    all_to_all x1, starting transfers between devices, local(): lax.all_to_all(jnp.stack([queries[0]] * lax.axis_size('seq')), 'seq', 0, 0)  14.9 us
    ppermute x2, starting transfers between devices, passed_along(): return lax.ppermute(block, axis, route)  14.9 us
  transfers between devices with their start and end apart: 7, of which 4 were waited for; matrix products, arithmetic and copies ran while one was open for 9% of the time, Pallas kernels for 0%

profile of v1, /device:TPU:97, one launch (start us, length us, event | category | flops | bytes accessed | tf_op | source)
XLA Modules:
  0.0 503.8 jit_solution(7822233720700263543)
XLA Ops:
  7.2 3.3 stack.32
  10.5 14.9 %all-to-all-start = ((bf16[32,128,512]{2,1,0:T(8,128)(2,1)}), bf16[32,128,512]{2,1,0:T(8,128)(2,1)}, u32[]{:S(2)}, u32[]{:S(2)}) async-start(bf16[32,128,512]{2,1,0:T(8,128)(2,1)} %stack.32), calls=%async_computation | async-start | bytes 8388608 | tf_op jit(solution)/shard_map/all_to_all | solution.py:61
  25.5 0.7 all-gather.3.cloned.1.call-update
  27.2 3.8 copy.83
  31.0 0.6 iota_reduce_fusion.1
  32.0 2.8 fusion.60
  34.7 146.4 %all-gather.3.cloned.1.call-done = bf16[1,4096,512]{2,1,0:T(8,128)(2,1)} async-done(((bf16[1,128,512]{2,1,0:T(8,128)(2,1)}), bf16[1,4096,512]{2,1,0:T(8,128)(2,1)}) %all-gather.3.cloned.1.call-update) | async-done | bytes 4194320 | tf_op jit(solution)/shard_map/all_gather | solution.py:63
  181.1 4.7 gather_fusion.6
  185.8 45.4 %all-to-all-done = bf16[32,128,512]{2,1,0:T(8,128)(2,1)} async-done(((bf16[32,128,512]{2,1,0:T(8,128)(2,1)}), bf16[32,128,512]{2,1,0:T(8,128)(2,1)}, u32[]{:S(2)}, u32[]{:S(2)}) %all-to-all-start) | async-done | bytes 4194336 | tf_op jit(solution)/shard_map/all_to_all | solution.py:61
  231.2 4.7 gather_fusion.5
  236.1 1.0 reshape.671
  237.0 0.9 reshape.667
  238.0 1.7 fusion.62
  239.7 3.2 fusion.9
  243.3 32.3 %all_gather.7 = f32[256,769]{1,0:T(8,128)S(1)} all-gather(f32[8,769]{1,0:T(8,128)S(1)} %pad_maximum_fusion.3), channel_id=1, replica_groups=mesh['grp'=4,'seq'=32,'mp'=4] {'seq'}, dimensions={0}, use_global_device_ids=true | all-gather | bytes 812064 | tf_op jit(solution)/shard_map/all_gather | solution.py:147
  275.7 0.7 iota_reduce_fusion
  276.5 1.1 copy.142
  277.9 0.6 gather_fusion
  278.7 0.7 copy.89
  279.4 8.8 %all-to-all-start.1 = ((f32[32,1,513]{2,1,0:T(1,128)}), f32[32,1,513]{2,1,0:T(1,128)S(1)}, u32[]{:S(2)}, u32[]{:S(2)}) async-start(f32[32,1,513]{2,1,0:T(1,128)} %copy.89), calls=%async_computation.1 | async-start | bytes 163840 | tf_op jit(solution)/shard_map/all_to_all | solution.py:43
  288.2 2.0 gather_fusion.2
  290.2 3.3 select_select_fusion
  293.6 0.9 slice.114
  294.5 1.7 gather_fusion.4
  296.6 3.4 all-to-all-done.1
  300.1 8.9 %all-to-all-start.2 = ((bf16[32,64,512]{2,1,0:T(8,128)(2,1)}), bf16[32,64,512]{2,1,0:T(8,128)(2,1)}, u32[]{:S(2)}, u32[]{:S(2)}) async-start(bf16[32,64,512]{2,1,0:T(8,128)(2,1)} %select_select_fusion), calls=%async_computation.2 | async-start | bytes 4194304 | tf_op jit(solution)/shard_map/all_to_all | solution.py:43
  309.3 1.9 fusion.3
  311.3 0.8 fusion.5
  312.3 2.4 broadcast_in_dim.191
  314.8 2.5 scatter_fusion
  317.7 0.8 copy-done.1
  318.5 0.9 fusion.61
  320.0 127.2 %psum.21 = f32[4,191]{1,0:T(4,128)S(1)} all-reduce(f32[4,191]{1,0:T(4,128)S(1)} %reduce_sum.58), channel_id=1, replica_groups=mesh['grp'=4,'seq'=32,'mp'=4] {'seq'}, use_global_device_ids=true, to_apply=%region_13.15 | all-reduce | flops 764 | bytes 6112 | tf_op jit(solution)/shard_map/psum | solution.py:189
  447.2 8.8 %psum.22 = f32[4,191]{1,0:T(4,128)S(1)} all-reduce(f32[4,191]{1,0:T(4,128)S(1)} %psum.21), channel_id=1, replica_groups=mesh['grp'=4,'seq'=32,'mp'=4] {'grp'}, use_global_device_ids=true, to_apply=%region_14.16 | all-reduce | flops 764 | bytes 6112 | tf_op jit(solution)/shard_map/psum | solution.py:189
  456.0 0.6 multiply_reduce_fusion.1
  456.6 9.1 %psum.23 = f32[]{:T(128)} all-reduce(f32[]{:T(128)} %multiply_reduce_fusion.1), channel_id=1, replica_groups=mesh['grp'=4,'seq'=32,'mp'=4] {'mp'}, use_global_device_ids=true, to_apply=%region_16.18 | all-reduce | flops 1 | bytes 8 | tf_op jit(solution)/shard_map/psum | solution.py:190
  467.3 0.9 multiply_convert_fusion
  468.1 3.8 copy.108
  471.9 0.6 broadcast_multiply_fusion
  472.6 0.7 iota_reduce_fusion.2
  474.5 2.2 gather_fusion.3
  477.5 9.4 %collective-permute-start = (bf16[64,512]{1,0:T(8,128)(2,1)S(1)}, bf16[64,512]{1,0:T(8,128)(2,1)S(1)}, u32[]{:S(2)}, u32[]{:S(2)}) collective-permute-start(bf16[64,512]{1,0:T(8,128)(2,1)S(1)} %bitcast.174), channel_id=1, source_target_pairs={{0,4},{4,8},{8,12},{12,16},{16,20},{20,24},{24,28},{28,32},{32,36}... | collective-permute-start | bytes 196616 | tf_op jit(solution)/shard_map/ppermute | solution.py:14
  487.1 1.2 collective-permute-done
  488.3 0.8 slice_bitcast_fusion.1
  489.2 5.5 %collective-permute-start.1 = (bf16[64,512]{1,0:T(8,128)(2,1)S(1)}, bf16[64,512]{1,0:T(8,128)(2,1)S(1)}, u32[]{:S(2)}, u32[]{:S(2)}) collective-permute-start(bf16[64,512]{1,0:T(8,128)(2,1)S(1)} %slice_bitcast_fusion.1), channel_id=1, source_target_pairs={{0,4},{4,8},{8,12},{12,16},{16,20},{20,24},{24,28},{28,32},{32,36}... | collective-permute-start | bytes 196616 | tf_op jit(solution)/shard_map/ppermute | solution.py:14
  494.6 0.7 maximum_bitcast_fusion
  495.3 0.9 slice.120
  496.2 0.7 maximum_bitcast_fusion.1
  (113 shorter events, 7.3 us)
Async XLA Ops:
  10.5 15.7 %copy-start.11 = (s32[1,8]{1,0:T(1,128)S(1)}, s32[1,8]{1,0:T(1,128)}, u32[]{:S(2)}) copy-start(s32[1,8]{1,0:T(1,128)} %param.11) | copy-start | bytes 100
  10.5 16.0 %copy-start.10 = (f32[4,191]{1,0:T(4,128)S(1)}, f32[4,191]{1,0:T(4,128)}, u32[]{:S(2)}) copy-start(f32[4,191]{1,0:T(4,128)} %param.12) | copy-start | bytes 9172
  10.5 220.6 %all-to-all-start = ((bf16[32,128,512]{2,1,0:T(8,128)(2,1)}), bf16[32,128,512]{2,1,0:T(8,128)(2,1)}, u32[]{:S(2)}, u32[]{:S(2)}) async-start(bf16[32,128,512]{2,1,0:T(8,128)(2,1)} %stack.32), calls=%async_computation | async-start | bytes 8388608 | tf_op jit(solution)/shard_map/all_to_all | solution.py:61
  25.5 1.7 copy-start.6
  25.5 155.6 %all-gather.3.cloned.1.call-start = ((), (), s32[]{:S(2)}) async-start(), calls=%async_computation.5 | async-start | bytes 4325376 | tf_op jit(solution)/shard_map/all_gather | solution.py:63
  236.0 3.6 copy-start.2
  238.0 1.7 copy-start.7
  275.6 0.9 copy-start.4
  279.4 20.7 %all-to-all-start.1 = ((f32[32,1,513]{2,1,0:T(1,128)}), f32[32,1,513]{2,1,0:T(1,128)S(1)}, u32[]{:S(2)}, u32[]{:S(2)}) async-start(f32[32,1,513]{2,1,0:T(1,128)} %copy.89), calls=%async_computation.1 | async-start | bytes 163840 | tf_op jit(solution)/shard_map/all_to_all | solution.py:43
  290.2 3.4 copy-start.5
  296.6 12.7 %copy-start.8 = (bf16[8,64,4,128]{3,2,1,0:T(4,128)(2,1)S(1)}, bf16[8,64,4,128]{3,2,1,0:T(4,128)(2,1)}, u32[]{:S(2)}) copy-start(bf16[8,64,4,128]{3,2,1,0:T(4,128)(2,1)} %reshape.671) | copy-start | bytes 1572868
  300.1 174.4 %all-to-all-start.2 = ((bf16[32,64,512]{2,1,0:T(8,128)(2,1)}), bf16[32,64,512]{2,1,0:T(8,128)(2,1)}, u32[]{:S(2)}, u32[]{:S(2)}) async-start(bf16[32,64,512]{2,1,0:T(8,128)(2,1)} %select_select_fusion), calls=%async_computation.2 | async-start | bytes 4194304 | tf_op jit(solution)/shard_map/all_to_all | solution.py:43
  309.0 179.3 %reduce-scatter.2.cloned.1.call-start = ((), (), s32[]{:S(2)}) async-start(), calls=%async_computation.4 | async-start | bytes 4325376 | tf_op jit(solution)/shard_map/reduce_scatter | solution.py:184
  311.3 1.0 copy-start
  317.3 1.2 copy-start.1
  317.3 148.4 %copy-start.3 = (bf16[512,512]{1,0:T(8,128)(2,1)S(1)}, bf16[512,512]{1,0:T(8,128)(2,1)}, u32[]{:S(2)}) copy-start(bf16[512,512]{1,0:T(8,128)(2,1)} %copy-done.2) | copy-start | bytes 1572868
  465.9 1.3 copy-start.9
  465.9 1.3 copy-start.12
  477.5 10.8 %collective-permute-start = (bf16[64,512]{1,0:T(8,128)(2,1)S(1)}, bf16[64,512]{1,0:T(8,128)(2,1)S(1)}, u32[]{:S(2)}, u32[]{:S(2)}) collective-permute-start(bf16[64,512]{1,0:T(8,128)(2,1)S(1)} %bitcast.174), channel_id=1, source_target_pairs={{0,4},{4,8},{8,12},{12,16},{16,20},{20,24},{24,28},{28,32},{32,36}... | collective-permute-start | bytes 196616 | tf_op jit(solution)/shard_map/ppermute | solution.py:14
  489.2 7.0 %collective-permute-start.1 = (bf16[64,512]{1,0:T(8,128)(2,1)S(1)}, bf16[64,512]{1,0:T(8,128)(2,1)S(1)}, u32[]{:S(2)}, u32[]{:S(2)}) collective-permute-start(bf16[64,512]{1,0:T(8,128)(2,1)S(1)} %slice_bitcast_fusion.1), channel_id=1, source_target_pairs={{0,4},{4,8},{8,12},{12,16},{16,20},{20,24},{24,28},{28,32},{32,36}... | collective-permute-start | bytes 196616 | tf_op jit(solution)/shard_map/ppermute | solution.py:14
Sparse Core Ops, SparseCore 0:
  28.4 152.5 all-gather.2
  317.4 154.2 reduce-scatter.1
